TPU v7x, 32 devices: a whole 2x2x4 slice. The times are simulated.
32 devices in a mesh: groups: 2 (over y), freq: 4 (over z), src: 2 (over x), vp: 2 (over core).
Axes of the slice: x: 2, y: 2, z: 4, core: 2. Of those that a mesh axis runs over, the one named last changes fastest.
Arguments:
- focus_direct: bfloat16 [4, 2, 192, 8192], P('freq', None, ('groups', 'vp'), 'src'), parts along dimension 2, may hold values from -6 to 6
- u_factors: bfloat16 [4, 32, 2, 32, 2048], P('freq', 'src'), may hold values from -0.1875 to 0.1875
- v_factors: bfloat16 [4, 8, 2, 32, 8192], P('freq', None, None, None, 'src'), may hold values from -0.375 to 0.375
- tile_ranks: int32 [4, 8, 32], P('freq', None, 'src'), may hold values from 16 to 32
- onset_rec: int32 [192, 2048], P(('groups', 'vp'), 'src'), parts along dimension 0, may hold values from 64 to 191
- onset_src: int32 [192, 8192], P(('groups', 'vp'), 'src'), parts along dimension 0, may hold values from 64 to 191
Outputs:
- focus_plus: bfloat16 [4, 2, 192, 8192], P('freq', None, ('groups', 'vp'), 'src'), parts along dimension 2
- focus_minus: bfloat16 [4, 2, 192, 2048], P('freq', None, ('groups', 'vp'), 'src'), parts along dimension 2
There are 2 independent parts, one for each index of `groups`. A program takes and returns all parts, laid end to end along the dimension named above; an argument that names none is the same for every part. Nothing has to cross between parts.
All inputs are finite; a program needn't handle non-finite values.
Results may differ from a plain program's by a relative error of at most 0.018.
Values may be sent and summed in bfloat16 or wider, within the bound.
No kernel may reach another device: no remote copies, remote signals or barrier semaphores. Data moves between devices by JAX's collectives and lax.ppermute only.
A program may use at most 128 MiB of HBM per device.

v0:
```python
import math
import jax
import jax.numpy as jnp
from jax import lax
from jax.sharding import PartitionSpec as P

TILE = 256
RANK = 32
NT = 256
FLO = 8
ITERS = 2


def make_tables(count):
    index = FLO + jnp.arange(count, dtype=jnp.int32)
    sample = jnp.arange(NT, dtype=jnp.int32)
    phase = (index[:, None] * sample[None, :] % NT).astype(jnp.float32) * (2.0 * math.pi / NT)
    cosine = jnp.cos(phase)
    sine = jnp.sin(phase)
    inverse = jnp.stack([cosine, -sine]) * (2.0 / NT)
    forward = jnp.stack([cosine, -sine])
    return (inverse, forward)


def window(spectrum, onset):
    inverse, forward = make_tables(spectrum.shape[0])
    signal = jnp.einsum("fcvm,cft->vmt", spectrum, inverse, precision=lax.Precision.HIGHEST)
    keep = jnp.arange(NT, dtype=jnp.int32)[None, None, :] < onset[:, :, None]
    signal = jnp.where(keep, signal, jnp.zeros_like(signal))
    return jnp.einsum("vmt,cft->fcvm", signal, forward, precision=lax.Precision.HIGHEST)


def coefficients(v_fac, mask, focus):
    points = focus.shape[1]
    row_tiles = v_fac.shape[0]
    col_tiles = v_fac.shape[-1] // TILE
    source = focus.reshape(2, points, col_tiles, TILE)
    v_tiles = v_fac.reshape(row_tiles, 2, RANK, col_tiles, TILE)
    form = "irjt,vjt->ivjr"
    z_real = jnp.einsum(
        form, v_tiles[:, 0], source[0], preferred_element_type=jnp.float32
    ) + jnp.einsum(form, v_tiles[:, 1], source[1], preferred_element_type=jnp.float32)
    z_imag = jnp.einsum(
        form, v_tiles[:, 0], source[1], preferred_element_type=jnp.float32
    ) - jnp.einsum(form, v_tiles[:, 1], source[0], preferred_element_type=jnp.float32)
    z_real = jnp.where(mask, z_real, 0.0).astype(jnp.bfloat16)
    z_imag = jnp.where(mask, z_imag, 0.0).astype(jnp.bfloat16)
    return jnp.stack([z_real, z_imag])


def expand_rows(u_fac, coeff):
    col_tiles = u_fac.shape[0]
    row_tiles = u_fac.shape[-1] // TILE
    points = coeff.shape[2]
    u_tiles = u_fac.reshape(col_tiles, 2, RANK, row_tiles, TILE)
    other = "jrit,ivjr->vit"
    y_real = jnp.einsum(
        other, u_tiles[:, 0], coeff[0], preferred_element_type=jnp.float32
    ) - jnp.einsum(other, u_tiles[:, 1], coeff[1], preferred_element_type=jnp.float32)
    y_imag = jnp.einsum(
        other, u_tiles[:, 0], coeff[1], preferred_element_type=jnp.float32
    ) + jnp.einsum(other, u_tiles[:, 1], coeff[0], preferred_element_type=jnp.float32)
    return jnp.stack([y_real.reshape(points, -1), y_imag.reshape(points, -1)])


def forward_local(u_fac, v_fac, mask, focus):
    return expand_rows(u_fac, coefficients(v_fac, mask, focus))


def adjoint_local(u_fac, v_fac, mask, focus):
    points = focus.shape[1]
    col_tiles = u_fac.shape[0]
    row_tiles = v_fac.shape[0]
    receiver = focus.reshape(2, points, row_tiles, TILE)
    v_tiles = v_fac.reshape(row_tiles, 2, RANK, col_tiles, TILE)
    u_tiles = u_fac.reshape(col_tiles, 2, RANK, row_tiles, TILE)
    form = "jrit,vit->ivjr"
    w_real = jnp.einsum(
        form, u_tiles[:, 0], receiver[0], preferred_element_type=jnp.float32
    ) + jnp.einsum(form, u_tiles[:, 1], receiver[1], preferred_element_type=jnp.float32)
    w_imag = jnp.einsum(
        form, u_tiles[:, 0], receiver[1], preferred_element_type=jnp.float32
    ) - jnp.einsum(form, u_tiles[:, 1], receiver[0], preferred_element_type=jnp.float32)
    w_real = jnp.where(mask, w_real, 0.0).astype(jnp.bfloat16)
    w_imag = jnp.where(mask, w_imag, 0.0).astype(jnp.bfloat16)
    other = "irjt,ivjr->vjt"
    x_real = jnp.einsum(
        other, v_tiles[:, 0], w_real, preferred_element_type=jnp.float32
    ) - jnp.einsum(other, v_tiles[:, 1], w_imag, preferred_element_type=jnp.float32)
    x_imag = jnp.einsum(
        other, v_tiles[:, 0], w_imag, preferred_element_type=jnp.float32
    ) + jnp.einsum(other, v_tiles[:, 1], w_real, preferred_element_type=jnp.float32)
    return jnp.stack([x_real.reshape(points, -1), x_imag.reshape(points, -1)])


def per_device(focus_direct, u_factors, v_factors, tile_ranks, onset_rec, onset_src):
    freq_count = lax.axis_size("freq")
    rank_index = jnp.arange(RANK, dtype=jnp.int32)
    masks = (rank_index[None, None, None, :] < tile_ranks[:, :, :, None])[:, :, None]
    rec_block = onset_rec.shape[1]
    rec_piece = rec_block // freq_count
    src_piece = onset_src.shape[1] // freq_count
    freq_place = lax.axis_index("freq")
    rec_onset = lax.dynamic_slice_in_dim(onset_rec, freq_place * rec_piece, rec_piece, 1)
    src_onset = lax.dynamic_slice_in_dim(onset_src, freq_place * src_piece, src_piece, 1)
    plus = focus_direct
    minus = None
    for sweep in range(ITERS):
        partial_terms = jax.vmap(forward_local)(u_factors, v_factors, masks, plus)
        summed = lax.psum_scatter(
            partial_terms.astype(jnp.bfloat16), "src", scatter_dimension=3, tiled=True
        ).astype(jnp.float32)
        traces = lax.all_to_all(
            summed.astype(jnp.bfloat16), "freq", split_axis=3, concat_axis=0, tiled=True
        ).astype(summed.dtype)
        windowed = window(traces, rec_onset).astype(jnp.bfloat16)
        minus = lax.all_to_all(windowed, "freq", split_axis=0, concat_axis=3, tiled=True)
        minus_all = lax.all_gather(minus, "src", axis=3, tiled=True)
        adjoint = jax.vmap(adjoint_local)(u_factors, v_factors, masks, minus_all)
        source_traces = lax.all_to_all(
            adjoint.astype(jnp.bfloat16), "freq", split_axis=3, concat_axis=0, tiled=True
        ).astype(adjoint.dtype)
        src_windowed = window(source_traces, src_onset)
        returned = lax.all_to_all(
            src_windowed.astype(jnp.bfloat16), "freq", split_axis=0, concat_axis=3, tiled=True
        ).astype(src_windowed.dtype)
        plus = (focus_direct.astype(jnp.float32) + returned).astype(jnp.bfloat16)
    return (plus, minus)


def solution(mesh):
    placed = (
        P("freq", None, ("groups", "vp"), "src"),
        P("freq", "src", None, None, None),
        P("freq", None, None, None, "src"),
        P("freq", None, "src"),
        P(("groups", "vp"), "src"),
        P(("groups", "vp"), "src"),
    )
    return jax.shard_map(
        per_device,
        mesh=mesh,
        in_specs=placed,
        out_specs=(
            P("freq", None, ("groups", "vp"), "src"),
            P("freq", None, ("groups", "vp"), "src"),
        ),
        check_vma=False,
    )
```

profile of v0, /device:TPU:0, one launch (start us, length us, event | category | flops | bytes accessed | tf_op | source)
XLA Modules:
  0.0 478.2 jit_solution(13236355608998709984)
XLA Ops:
  7.2 1.4 copy.194
  8.7 3.6 copy.195
  12.3 3.3 slice_bitcast_fusion.2
  16.3 2.1 fusion.160
  18.4 2.1 fusion.159
  21.2 2.1 fusion.158
  23.3 2.1 fusion.161
  25.5 3.7 copy.196
  29.2 3.2 slice_bitcast_fusion
  32.4 1.6 copy-done.18
  34.9 1.4 fusion.151
  41.8 15.2 %reduce-scatter.3.cloned.1.call-done = bf16[1,2,48,1024]{3,2,1,0:T(8,128)(2,1)} async-done(((bf16[1,2,48,2048]{3,2,1,0:T(8,128)(2,1)}), bf16[1,2,48,1024]{3,2,1,0:T(8,128)(2,1)}) %reduce-scatter.3.cloned.1.call-update) | async-done | bytes 196624 | tf_op jit(solution)/shard_map/reduce_scatter | solution.py:110
  58.2 1.5 reshape.568
  59.7 4.6 all-to-all-start
  64.4 7.4 %all-to-all-done = bf16[4,2,12288]{2,1,0:T(2,128)(2,1)} async-done(((bf16[4,2,12288]{2,1,0:T(2,128)(2,1)}), bf16[4,2,12288]{2,1,0:T(2,128)(2,1)}, u32[]{:S(2)}, u32[]{:S(2)}) %all-to-all-start) | async-done | bytes 196640 | tf_op jit(solution)/shard_map/all_to_all | solution.py:113
  71.8 1.4 reshape.569
  74.3 6.0 %fusion.168 = f32[48,256,256,1]{2,1,0,3:T(8,128)S(1)} fusion(bf16[1,2,48,4,256]{4,3,2,1,0:T(4,128)(2,1)} %copy.170, f32[1,4,256]{2,1,0:T(4,128)S(1)} %get-tuple-element.27, f32[1,4,256]{2,1,0:T(4,128)S(1)} %get-tuple-element.26), kind=kOutput, calls=%fused_computation.144 | convolution fusion | flops 301993984 | bytes 12787712 | tf_op jit(solution)/shard_map/fcvm,cft->vmt/dot_general | solution.py:27
  80.3 12.0 %fusion.143 = bf16[4,2,48,256]{3,0,2,1:T(4,128)(2,1)S(1)} fusion(f32[48,256,256,1]{2,1,0,3:T(8,128)S(1)} %fusion.168, s32[48,256]{1,0:T(8,128)S(1)} %constant_dynamic-slice_fusion, f32[1,4,256]{2,1,0:T(4,128)S(1)} %get-tuple-element.27, f32[1,4,256]{2,1,0:T(4,128)S(1)} %get-tuple-element.26), kind=kOutput, calls=%fused_computation.109 | convolution fusion | flops 308381696 | bytes 12836864 | tf_op jit(solution)/shard_map/vmt,cft->fcvm/dot_general | solution.py:30
  93.1 3.6 all-to-all-start.1
  96.7 3.6 copy.131
  100.3 1.9 copy.129
  102.9 6.5 %all_gather.6 = bf16[1,2,48,2048]{3,2,1,0:T(8,128)(2,1)S(1)} all-gather(bf16[1,2,48,1024]{3,2,1,0:T(8,128)(2,1)S(1)} %bitcast.606), channel_id=1, replica_groups=mesh['groups'=2,'freq'=4,'src'=2,'vp'=2] {'src'}, dimensions={3}, use_global_device_ids=true | all-gather | bytes 589824 | tf_op jit(solution)/shard_map/all_gather | solution.py:118
  119.7 1.9 reshape.493
  123.7 1.9 maximum_bitcast_fusion
  125.6 5.4 %copy.140 = bf16[1,2,48,4096]{2,1,0,3:T(2,128)(2,1)} copy(bf16[1,2,48,4096]{3,2,1,0:T(8,128)(2,1)} %maximum_bitcast_fusion) | data formatting | bytes 1572864 | tf_op jit(solution)/shard_map/convert_element_type | solution.py:121
  131.1 5.1 %reshape.570 = bf16[4,2,49152]{2,1,0:T(2,128)(2,1)} reshape(bf16[4096,1,2,48]{3,2,1,0:T(2,128)(2,1)} %bitcast.582) | data formatting | bytes 1572864
  136.2 4.3 all-to-all-start.2
  140.6 17.3 %all-to-all-done.2 = bf16[4,2,49152]{2,1,0:T(2,128)(2,1)} async-done(((bf16[4,2,49152]{2,1,0:T(2,128)(2,1)}), bf16[4,2,49152]{2,1,0:T(2,128)(2,1)}, u32[]{:S(2)}, u32[]{:S(2)}) %all-to-all-start.2) | async-done | bytes 786464 | tf_op jit(solution)/shard_map/all_to_all | solution.py:120
  157.9 4.9 %reshape.571 = bf16[4096,1,2,48]{3,2,1,0:T(2,128)(2,1)} reshape(bf16[4,2,49152]{2,1,0:T(2,128)(2,1)} %all-to-all-done.2) | data formatting | bytes 1572864
  162.8 5.0 %copy.171 = bf16[1,2,48,4,1024]{4,3,2,1,0:T(4,128)(2,1)S(1)} copy(bf16[1,2,48,4,1024]{2,1,4,3,0:T(2,128)(2,1)} %bitcast.583) | data formatting | bytes 1572864 | tf_op jit(solution)/shard_map/all_to_all | solution.py:120
  167.8 24.2 %fusion.156 = f32[48,1024,256,1]{2,1,0,3:T(8,128)} fusion(bf16[1,2,48,4,1024]{4,3,2,1,0:T(4,128)(2,1)S(1)} %copy.171, f32[1,4,256]{2,1,0:T(4,128)S(1)} %get-tuple-element.27, f32[1,4,256]{2,1,0:T(4,128)S(1)} %get-tuple-element.26), kind=kOutput, calls=%fused_computation.122 | convolution fusion | flops 1207963648 | bytes 51126272 | tf_op jit(solution)/shard_map/fcvm,cft->vmt/dot_general | solution.py:27
  192.1 46.6 %fusion.79 = bf16[4,2,48,1024]{3,0,2,1:T(4,128)(2,1)S(1)} fusion(f32[48,1024,256,1]{2,1,0,3:T(8,128)} %fusion.156, s32[48,1024]{1,0:T(8,128)S(1)} %constant_dynamic-slice_fusion.1, f32[1,4,256]{2,1,0:T(4,128)S(1)} %get-tuple-element.27, f32[1,4,256]{2,1,0:T(4,128)S(1)} %get-tuple-element.26), kind=kOutput, calls=%fused_computation.77 | convolution fusion | flops 1233520640 | bytes 51322880 | tf_op jit(solution)/shard_map/vmt,cft->fcvm/dot_general | solution.py:30
  238.9 20.7 %all_to_all.126 = bf16[4,2,48,1024]{3,2,1,0:T(8,128)(2,1)S(1)} all-to-all(bf16[4,2,48,1024]{3,2,1,0:T(8,128)(2,1)S(1)} %copy.142), channel_id=1, replica_groups=mesh['groups'=2,'freq'=4,'src'=2,'vp'=2] {'freq'}, dimensions={0} | all-to-all | bytes 1572864 | tf_op jit(solution)/shard_map/all_to_all | solution.py:124
  272.6 11.4 %reduce-scatter.5.cloned.1.call-done = bf16[1,2,48,1024]{3,2,1,0:T(8,128)(2,1)} async-done(((bf16[1,2,48,2048]{3,2,1,0:T(8,128)(2,1)}), bf16[1,2,48,1024]{3,2,1,0:T(8,128)(2,1)}) %reduce-scatter.5.cloned.1.call-update) | async-done | bytes 196624 | tf_op jit(solution)/shard_map/reduce_scatter | solution.py:110
  286.0 12.1 %all_to_all.127 = bf16[4,2,12288]{2,1,0:T(2,128)(2,1)S(1)} all-to-all(bf16[4,2,12288]{2,1,0:T(2,128)(2,1)S(1)} %reshape.572), channel_id=1, replica_groups=mesh['groups'=2,'freq'=4,'src'=2,'vp'=2] {'freq'}, dimensions={0} | all-to-all | bytes 393216 | tf_op jit(solution)/shard_map/all_to_all | solution.py:113
  299.1 5.1 %fusion.166 = f32[48,256,256,1]{2,1,0,3:T(8,128)S(1)} fusion(bf16[1,2,48,4,256]{4,3,2,1,0:T(4,128)(2,1)S(1)} %copy.172, f32[1,4,256]{2,1,0:T(4,128)S(1)} %get-tuple-element.27, f32[1,4,256]{2,1,0:T(4,128)S(1)} %get-tuple-element.26), kind=kOutput, calls=%fused_computation.142 | convolution fusion | flops 301993984 | bytes 12787712 | tf_op jit(solution)/shard_map/fcvm,cft->vmt/dot_general | solution.py:27
  304.2 12.0 %fusion.140 = bf16[4,2,48,256]{3,0,2,1:T(4,128)(2,1)S(1)} fusion(f32[48,256,256,1]{2,1,0,3:T(8,128)S(1)} %fusion.166, s32[48,256]{1,0:T(8,128)S(1)} %constant_dynamic-slice_fusion, f32[1,4,256]{2,1,0:T(4,128)S(1)} %get-tuple-element.27, f32[1,4,256]{2,1,0:T(4,128)S(1)} %get-tuple-element.26), kind=kOutput, calls=%fused_computation.108 | convolution fusion | flops 308381696 | bytes 12836864 | tf_op jit(solution)/shard_map/vmt,cft->fcvm/dot_general | solution.py:30
  316.3 10.0 %all_to_all.128 = bf16[4,2,48,256]{3,2,1,0:T(8,128)(2,1)S(1)} all-to-all(bf16[4,2,48,256]{3,2,1,0:T(8,128)(2,1)S(1)} %copy.150), channel_id=1, replica_groups=mesh['groups'=2,'freq'=4,'src'=2,'vp'=2] {'freq'}, dimensions={0} | all-to-all | bytes 393216 | tf_op jit(solution)/shard_map/all_to_all | solution.py:117
  326.3 6.3 %all_gather.7 = bf16[1,2,48,2048]{3,2,1,0:T(8,128)(2,1)S(1)} all-gather(bf16[1,2,48,1024]{3,2,1,0:T(8,128)(2,1)S(1)} %bitcast.604), channel_id=1, replica_groups=mesh['groups'=2,'freq'=4,'src'=2,'vp'=2] {'src'}, dimensions={3}, use_global_device_ids=true | all-gather | bytes 589824 | tf_op jit(solution)/shard_map/all_gather | solution.py:118
  336.5 1.5 select_convert_fusion.1
  342.9 2.8 copy.164
  345.7 3.3 reshape.574
  349.0 21.8 %all_to_all.129 = bf16[4,2,49152]{2,1,0:T(2,128)(2,1)} all-to-all(bf16[4,2,49152]{2,1,0:T(2,128)(2,1)S(1)} %reshape.574), channel_id=1, replica_groups=mesh['groups'=2,'freq'=4,'src'=2,'vp'=2] {'freq'}, dimensions={0} | all-to-all | bytes 1572864 | tf_op jit(solution)/shard_map/all_to_all | solution.py:120
  370.8 3.4 reshape.575
  374.3 1.6 copy.173
  375.9 24.2 %fusion.154 = f32[48,1024,256,1]{2,1,0,3:T(8,128)} fusion(bf16[1,2,48,4,1024]{4,3,2,1,0:T(4,128)(2,1)S(1)} %copy.173, f32[1,4,256]{2,1,0:T(4,128)S(1)} %get-tuple-element.27, f32[1,4,256]{2,1,0:T(4,128)S(1)} %get-tuple-element.26), kind=kOutput, calls=%fused_computation.120 | convolution fusion | flops 1207963648 | bytes 51126272 | tf_op jit(solution)/shard_map/fcvm,cft->vmt/dot_general | solution.py:27
  400.1 46.6 %fusion.76 = bf16[4,2,48,1024]{3,0,2,1:T(4,128)(2,1)S(1)} fusion(f32[48,1024,256,1]{2,1,0,3:T(8,128)} %fusion.154, s32[48,1024]{1,0:T(8,128)S(1)} %constant_dynamic-slice_fusion.1, f32[1,4,256]{2,1,0:T(4,128)S(1)} %get-tuple-element.27, f32[1,4,256]{2,1,0:T(4,128)S(1)} %get-tuple-element.26), kind=kOutput, calls=%fused_computation.76 | convolution fusion | flops 1233520640 | bytes 51322880 | tf_op jit(solution)/shard_map/vmt,cft->fcvm/dot_general | solution.py:30
  447.0 21.5 %all_to_all.130 = bf16[4,2,48,1024]{3,2,1,0:T(8,128)(2,1)S(1)} all-to-all(bf16[4,2,48,1024]{3,2,1,0:T(8,128)(2,1)S(1)} %copy.166), channel_id=1, replica_groups=mesh['groups'=2,'freq'=4,'src'=2,'vp'=2] {'freq'}, dimensions={0} | all-to-all | bytes 1572864 | tf_op jit(solution)/shard_map/all_to_all | solution.py:124
  (136 shorter events, 51.5 us)
Async XLA Ops:
  7.2 133.4 %copy-start = (s32[48,4096]{1,0:T(8,128)S(1)}, s32[48,4096]{1,0:T(8,128)}, u32[]{:S(2)}) copy-start(s32[48,4096]{1,0:T(8,128)} %param.11) | copy-start | bytes 2359300
  7.2 49.7 %reduce-scatter.3.cloned.1.call-start = ((), (), s32[]{:S(2)}) async-start(), calls=%async_computation.10 | async-start | bytes 589824 | tf_op jit(solution)/shard_map/reduce_scatter | solution.py:110
  16.3 2.1 copy-start.2
  21.2 2.1 copy-start.4
  23.3 2.1 copy-start.24
  29.2 3.2 copy-start.16
  29.2 3.2 copy-start.17
  29.2 4.8 copy-start.18
  29.2 5.7 %copy-start.19 = (f32[16,48,256]{1,2,0:S(1)}, f32[16,48,256]{1,2,0}, u32[]{:S(2)}) copy-start(f32[16,48,256]{1,2,0} %fusion.161) | copy-start | bytes 2359300
  32.4 4.8 %copy-start.6 = (bf16[1,16,1,32,8,256]{5,4,3,2,1,0:T(8,128)(2,1)}, bf16[1,16,1,32,8,256]{5,4,3,2,1,0:T(8,128)(2,1)S(1)}, u32[]{:S(2)}) copy-start(bf16[1,16,1,32,8,256]{5,4,3,2,1,0:T(8,128)(2,1)S(1)} %get-tuple-element.9) | copy-start | bytes 6291460
  59.7 12.2 %all-to-all-start = ((bf16[4,2,12288]{2,1,0:T(2,128)(2,1)}), bf16[4,2,12288]{2,1,0:T(2,128)(2,1)}, u32[]{:S(2)}, u32[]{:S(2)}) async-start(bf16[4,2,12288]{2,1,0:T(2,128)(2,1)} %reshape.568), calls=%async_computation.1 | async-start | bytes 393216 | tf_op jit(solution)/shard_map/all_to_all | solution.py:113
  93.1 9.8 %all-to-all-start.1 = ((bf16[4,2,48,256]{3,2,1,0:T(8,128)(2,1)}), bf16[4,2,48,256]{3,2,1,0:T(8,128)(2,1)S(1)}, u32[]{:S(2)}, u32[]{:S(2)}) async-start(bf16[4,2,48,256]{3,2,1,0:T(8,128)(2,1)} %copy.126), calls=%async_computation.2 | async-start | bytes 393216 | tf_op jit(solution)/shard_map/all_to_all | solution.py:117
  96.7 3.6 copy-start.20
  102.9 6.6 %copy-start.8 = (bf16[16,32,8,256]{3,1,0,2:T(8,128)(2,1)S(1)}, bf16[16,32,8,256]{3,1,0,2:T(8,128)(2,1)}, u32[]{:S(2)}) copy-start(bf16[16,32,8,256]{3,1,0,2:T(8,128)(2,1)} %copy.131) | copy-start | bytes 6291460
  109.5 1.6 copy-start.10
  113.2 1.6 copy-start.14
  115.6 1.6 copy-start.12
  136.2 21.7 %all-to-all-start.2 = ((bf16[4,2,49152]{2,1,0:T(2,128)(2,1)}), bf16[4,2,49152]{2,1,0:T(2,128)(2,1)}, u32[]{:S(2)}, u32[]{:S(2)}) async-start(bf16[4,2,49152]{2,1,0:T(2,128)(2,1)} %reshape.570), calls=%async_computation.3 | async-start | bytes 1572864 | tf_op jit(solution)/shard_map/all_to_all | solution.py:120
  140.6 143.4 %reduce-scatter.5.cloned.1.call-start = ((), (), s32[]{:S(2)}) async-start(), calls=%async_computation.11 | async-start | bytes 589824 | tf_op jit(solution)/shard_map/reduce_scatter | solution.py:110
  259.8 1.1 copy-start.21
  261.1 1.6 copy-start.3
  262.7 1.6 copy-start.5
  266.4 1.6 copy-start.7
  316.2 16.6 %copy-start.9 = (bf16[16,32,8,256]{3,1,0,2:T(8,128)(2,1)S(1)}, bf16[16,32,8,256]{3,1,0,2:T(8,128)(2,1)}, u32[]{:S(2)}) copy-start(bf16[16,32,8,256]{3,1,0,2:T(8,128)(2,1)} %copy.131) | copy-start | bytes 6291460
  326.3 6.4 %copy-start.23 = (bf16[1,4,2,6,8,256]{5,4,1,3,2,0:T(8,128)(2,1)}, bf16[1,4,2,6,8,256]{5,4,1,3,2,0:T(8,128)(2,1)S(1)}, u32[]{:S(2)}) copy-start(bf16[1,4,2,6,8,256]{5,4,1,3,2,0:T(8,128)(2,1)S(1)} %copy.192) | copy-start | bytes 589828
  332.8 1.6 copy-start.11
  336.5 1.6 copy-start.15
  338.9 1.6 copy-start.13
  468.7 1.1 copy-start.22
  468.7 2.2 copy-start.1
Sparse Core Ops, SparseCore 0:
  41.1 15.7 reduce-scatter.2
  272.7 11.1 reduce-scatter.4
where the time goes:
time: 486 us; the launch traced here: 478 us
  matrix products  207 us (43%)
  blocking collectives  99 us (20%)
  local copies, waits for them, and re-layouts  81.7 us (17%)
  waiting for transfers between devices  52 us (11%)
  between operations  15.2 us (3%)
  starting transfers between devices  12.6 us (3%)
  other arithmetic  10.8 us (2%)
    dot_general x4, matrix products, window(): jnp.einsum('vmt,cft->fcvm', signal, forward, precision=lax.Precision.HIGH...  117 us
    dot_general x4, matrix products, window(): jnp.einsum('fcvm,cft->vmt', spectrum, inverse, precision=lax.Precision.HI...  59.6 us
    unnamed x66, local copies, waits for them, and re-layouts  42.3 us
    all_to_all x2, blocking collectives, per_device(): lax.all_to_all(src_windowed.astype(jnp.bfloat16), 'freq', split_axis=0, c...  42.2 us
    reduce_scatter x2, waiting for transfers between devices, per_device(): lax.psum_scatter(partial_terms.astype(jnp.bfloat16), 'src', scatter_dimen...  26.5 us
    all_to_all x1, blocking collectives, per_device(): lax.all_to_all(adjoint.astype(jnp.bfloat16), 'freq', split_axis=3, concat...  21.8 us
    all_to_all x1, waiting for transfers between devices, per_device(): lax.all_to_all(adjoint.astype(jnp.bfloat16), 'freq', split_axis=3, concat...  17.3 us
    unnamed x16, matrix products  16.6 us
  transfers between devices with their start and end apart: 5, of which 5 were waited for; matrix products, arithmetic and copies ran while one was open for 1% of the time, Pallas kernels for 0%

commit v1 on v0

--- a/solution.py
+++ b/solution.py
@@ -121,9 +121,15 @@
             adjoint.astype(jnp.bfloat16), "freq", split_axis=3, concat_axis=0, tiled=True
         ).astype(adjoint.dtype)
         src_windowed = window(source_traces, src_onset)
-        returned = lax.all_to_all(
-            src_windowed.astype(jnp.bfloat16), "freq", split_axis=0, concat_axis=3, tiled=True
-        ).astype(src_windowed.dtype)
+        _register_tasks = lambda mat, mesh_dim: jnp.concatenate(
+            lax.all_to_all(
+                jnp.stack(jnp.split(mat, lax.axis_size(mesh_dim), 0), axis=0), mesh_dim, 0, 0
+            ),
+            3,
+        )
+        returned = _register_tasks(src_windowed.astype(jnp.bfloat16), "freq").astype(
+            src_windowed.dtype
+        )
         plus = (focus_direct.astype(jnp.float32) + returned).astype(jnp.bfloat16)
     return (plus, minus)
 

time: 486 us -> 489 us (level)
    unnamed x66 -> x72, local copies, waits for them, and re-layouts: 42.3 us -> 42.7 us
where the time goes in v1:
time: 489 us; the launch traced here: 481 us
  matrix products  207 us (42%)
  blocking collectives  99.5 us (20%)
  local copies, waits for them, and re-layouts  83.9 us (17%)
  waiting for transfers between devices  52 us (11%)
  between operations  15.1 us (3%)
  starting transfers between devices  12.6 us (3%)
  other arithmetic  11.2 us (2%)
    dot_general x4, matrix products, window(): jnp.einsum('vmt,cft->fcvm', signal, forward, precision=lax.Precision.HIGH...  117 us
    dot_general x4, matrix products, window(): jnp.einsum('fcvm,cft->vmt', spectrum, inverse, precision=lax.Precision.HI...  59.5 us
    unnamed x72, local copies, waits for them, and re-layouts  42.7 us
    all_to_all x2, blocking collectives, per_device(): lax.all_to_all(jnp.stack(jnp.split(mat, lax.axis_size(mesh_dim), 0), axis...  42.3 us
    reduce_scatter x2, waiting for transfers between devices, per_device(): lax.psum_scatter(partial_terms.astype(jnp.bfloat16), 'src', scatter_dimen...  26.5 us
    all_to_all x1, blocking collectives, per_device(): lax.all_to_all(adjoint.astype(jnp.bfloat16), 'freq', split_axis=3, concat...  22 us
    all_to_all x1, waiting for transfers between devices, per_device(): lax.all_to_all(adjoint.astype(jnp.bfloat16), 'freq', split_axis=3, concat...  17.2 us
    unnamed x16, matrix products  16.5 us
  transfers between devices with their start and end apart: 5, of which 5 were waited for; matrix products, arithmetic and copies ran while one was open for 1% of the time, Pallas kernels for 0%

profile of v1, /device:TPU:0, one launch (start us, length us, event | category | flops | bytes accessed | tf_op | source)
XLA Modules:
  0.0 481.0 jit_solution(3658555383796290127)
XLA Ops:
  7.2 1.4 copy.334
  8.7 3.6 copy.335
  12.3 3.3 slice_bitcast_fusion.2
  16.3 2.1 fusion.160
  18.4 2.1 fusion.159
  21.2 2.0 fusion.158
  23.2 2.1 fusion.161
  25.5 3.7 copy.336
  29.2 3.2 slice_bitcast_fusion
  32.4 1.6 copy-done.18
  34.9 1.6 fusion.151
  42.0 15.2 %reduce-scatter.3.cloned.1.call-done = bf16[1,2,48,1024]{3,2,1,0:T(8,128)(2,1)} async-done(((bf16[1,2,48,2048]{3,2,1,0:T(8,128)(2,1)}), bf16[1,2,48,1024]{3,2,1,0:T(8,128)(2,1)}) %reduce-scatter.3.cloned.1.call-update) | async-done | bytes 196624 | tf_op jit(solution)/shard_map/reduce_scatter | solution.py:110
  58.4 1.5 reshape.566
  59.9 4.6 all-to-all-start
  64.6 7.5 %all-to-all-done = bf16[4,2,12288]{2,1,0:T(2,128)(2,1)} async-done(((bf16[4,2,12288]{2,1,0:T(2,128)(2,1)}), bf16[4,2,12288]{2,1,0:T(2,128)(2,1)}, u32[]{:S(2)}, u32[]{:S(2)}) %all-to-all-start) | async-done | bytes 196640 | tf_op jit(solution)/shard_map/all_to_all | solution.py:113
  72.1 1.4 reshape.567
  74.6 6.0 %fusion.168 = f32[48,256,256,1]{2,1,0,3:T(8,128)S(1)} fusion(bf16[1,2,48,4,256]{4,3,2,1,0:T(4,128)(2,1)} %copy.302, f32[1,4,256]{2,1,0:T(4,128)S(1)} %get-tuple-element.35, f32[1,4,256]{2,1,0:T(4,128)S(1)} %get-tuple-element.34), kind=kOutput, calls=%fused_computation.154 | convolution fusion | flops 301993984 | bytes 12787712 | tf_op jit(solution)/shard_map/fcvm,cft->vmt/dot_general | solution.py:27
  80.6 12.0 %fusion.143 = bf16[4,2,48,256]{3,0,2,1:T(4,128)(2,1)S(1)} fusion(f32[48,256,256,1]{2,1,0,3:T(8,128)S(1)} %fusion.168, s32[48,256]{1,0:T(8,128)S(1)} %constant_dynamic-slice_fusion, f32[1,4,256]{2,1,0:T(4,128)S(1)} %get-tuple-element.35, f32[1,4,256]{2,1,0:T(4,128)S(1)} %get-tuple-element.34), kind=kOutput, calls=%fused_computation.109 | convolution fusion | flops 308381696 | bytes 12836864 | tf_op jit(solution)/shard_map/vmt,cft->fcvm/dot_general | solution.py:30
  93.4 3.5 all-to-all-start.1
  96.9 3.6 copy.265
  100.6 1.9 copy.263
  103.1 6.5 %all_gather.6 = bf16[1,2,48,2048]{3,2,1,0:T(8,128)(2,1)S(1)} all-gather(bf16[1,2,48,1024]{3,2,1,0:T(8,128)(2,1)S(1)} %bitcast.624), channel_id=1, replica_groups=mesh['groups'=2,'freq'=4,'src'=2,'vp'=2] {'src'}, dimensions={3}, use_global_device_ids=true | all-gather | bytes 589824 | tf_op jit(solution)/shard_map/all_gather | solution.py:118
  119.9 1.9 reshape.493
  123.9 1.9 maximum_bitcast_fusion
  125.9 5.4 %copy.274 = bf16[1,2,48,4096]{2,1,0,3:T(2,128)(2,1)} copy(bf16[1,2,48,4096]{3,2,1,0:T(8,128)(2,1)} %maximum_bitcast_fusion) | data formatting | bytes 1572864 | tf_op jit(solution)/shard_map/convert_element_type | solution.py:121
  131.3 5.1 %reshape.568 = bf16[4,2,49152]{2,1,0:T(2,128)(2,1)} reshape(bf16[4096,1,2,48]{3,2,1,0:T(2,128)(2,1)} %bitcast.596) | data formatting | bytes 1572864
  136.4 4.4 all-to-all-start.2
  140.8 17.2 %all-to-all-done.2 = bf16[4,2,49152]{2,1,0:T(2,128)(2,1)} async-done(((bf16[4,2,49152]{2,1,0:T(2,128)(2,1)}), bf16[4,2,49152]{2,1,0:T(2,128)(2,1)}, u32[]{:S(2)}, u32[]{:S(2)}) %all-to-all-start.2) | async-done | bytes 786464 | tf_op jit(solution)/shard_map/all_to_all | solution.py:120
  158.1 4.7 reshape.569
  162.7 5.0 %copy.303 = bf16[1,2,48,4,1024]{4,3,2,1,0:T(4,128)(2,1)S(1)} copy(bf16[1,2,48,4,1024]{2,1,4,3,0:T(2,128)(2,1)} %bitcast.597) | data formatting | bytes 1572864 | tf_op jit(solution)/shard_map/all_to_all | solution.py:120
  167.8 24.2 %fusion.156 = f32[48,1024,256,1]{2,1,0,3:T(8,128)} fusion(bf16[1,2,48,4,1024]{4,3,2,1,0:T(4,128)(2,1)S(1)} %copy.303, f32[1,4,256]{2,1,0:T(4,128)S(1)} %get-tuple-element.35, f32[1,4,256]{2,1,0:T(4,128)S(1)} %get-tuple-element.34), kind=kOutput, calls=%fused_computation.124 | convolution fusion | flops 1207963648 | bytes 51126272 | tf_op jit(solution)/shard_map/fcvm,cft->vmt/dot_general | solution.py:27
  192.0 46.6 %fusion.79 = bf16[4,2,48,1024]{3,0,2,1:T(4,128)(2,1)S(1)} fusion(f32[48,1024,256,1]{2,1,0,3:T(8,128)} %fusion.156, s32[48,1024]{1,0:T(8,128)S(1)} %constant_dynamic-slice_fusion.1, f32[1,4,256]{2,1,0:T(4,128)S(1)} %get-tuple-element.35, f32[1,4,256]{2,1,0:T(4,128)S(1)} %get-tuple-element.34), kind=kOutput, calls=%fused_computation.77 | convolution fusion | flops 1233520640 | bytes 51322880 | tf_op jit(solution)/shard_map/vmt,cft->fcvm/dot_general | solution.py:30
  240.2 20.7 %all_to_all.118 = bf16[4,1,2,48,1024]{4,3,2,1,0:T(8,128)(2,1)S(1)} all-to-all(bf16[4,1,2,48,1024]{4,3,2,1,0:T(8,128)(2,1)S(1)} %pad_maximum_fusion), channel_id=1, replica_groups=mesh['groups'=2,'freq'=4,'src'=2,'vp'=2] {'freq'}, dimensions={0} | all-to-all | bytes 1572864 | tf_op jit(solution)/shard_map/all_to_all | solution.py:125
  273.9 11.4 %reduce-scatter.5.cloned.1.call-done = bf16[1,2,48,1024]{3,2,1,0:T(8,128)(2,1)} async-done(((bf16[1,2,48,2048]{3,2,1,0:T(8,128)(2,1)}), bf16[1,2,48,1024]{3,2,1,0:T(8,128)(2,1)}) %reduce-scatter.5.cloned.1.call-update) | async-done | bytes 196624 | tf_op jit(solution)/shard_map/reduce_scatter | solution.py:110
  287.3 12.3 %all_to_all.119 = bf16[4,2,12288]{2,1,0:T(2,128)(2,1)S(1)} all-to-all(bf16[4,2,12288]{2,1,0:T(2,128)(2,1)S(1)} %reshape.570), channel_id=1, replica_groups=mesh['groups'=2,'freq'=4,'src'=2,'vp'=2] {'freq'}, dimensions={0} | all-to-all | bytes 393216 | tf_op jit(solution)/shard_map/all_to_all | solution.py:113
  300.6 5.1 %fusion.166 = f32[48,256,256,1]{2,1,0,3:T(8,128)S(1)} fusion(bf16[1,2,48,4,256]{4,3,2,1,0:T(4,128)(2,1)S(1)} %copy.304, f32[1,4,256]{2,1,0:T(4,128)S(1)} %get-tuple-element.35, f32[1,4,256]{2,1,0:T(4,128)S(1)} %get-tuple-element.34), kind=kOutput, calls=%fused_computation.152 | convolution fusion | flops 301993984 | bytes 12787712 | tf_op jit(solution)/shard_map/fcvm,cft->vmt/dot_general | solution.py:27
  305.7 12.0 %fusion.140 = bf16[4,2,48,256]{3,0,2,1:T(4,128)(2,1)S(1)} fusion(f32[48,256,256,1]{2,1,0,3:T(8,128)S(1)} %fusion.166, s32[48,256]{1,0:T(8,128)S(1)} %constant_dynamic-slice_fusion, f32[1,4,256]{2,1,0:T(4,128)S(1)} %get-tuple-element.35, f32[1,4,256]{2,1,0:T(4,128)S(1)} %get-tuple-element.34), kind=kOutput, calls=%fused_computation.108 | convolution fusion | flops 308381696 | bytes 12836864 | tf_op jit(solution)/shard_map/vmt,cft->fcvm/dot_general | solution.py:30
  317.8 10.0 %all_to_all.120 = bf16[4,2,48,256]{3,2,1,0:T(8,128)(2,1)S(1)} all-to-all(bf16[4,2,48,256]{3,2,1,0:T(8,128)(2,1)S(1)} %copy.283), channel_id=1, replica_groups=mesh['groups'=2,'freq'=4,'src'=2,'vp'=2] {'freq'}, dimensions={0} | all-to-all | bytes 393216 | tf_op jit(solution)/shard_map/all_to_all | solution.py:117
  327.9 6.3 %all_gather.7 = bf16[1,2,48,2048]{3,2,1,0:T(8,128)(2,1)S(1)} all-gather(bf16[1,2,48,1024]{3,2,1,0:T(8,128)(2,1)S(1)} %bitcast.622), channel_id=1, replica_groups=mesh['groups'=2,'freq'=4,'src'=2,'vp'=2] {'src'}, dimensions={3}, use_global_device_ids=true | all-gather | bytes 589824 | tf_op jit(solution)/shard_map/all_gather | solution.py:118
  338.0 1.4 select_convert_fusion.1
  344.4 2.8 copy.297
  347.2 3.3 reshape.572
  350.5 22.0 %all_to_all.121 = bf16[4,2,49152]{2,1,0:T(2,128)(2,1)} all-to-all(bf16[4,2,49152]{2,1,0:T(2,128)(2,1)S(1)} %reshape.572), channel_id=1, replica_groups=mesh['groups'=2,'freq'=4,'src'=2,'vp'=2] {'freq'}, dimensions={0} | all-to-all | bytes 1572864 | tf_op jit(solution)/shard_map/all_to_all | solution.py:120
  372.6 3.4 reshape.573
  376.0 1.6 copy.305
  377.6 24.2 %fusion.154 = f32[48,1024,256,1]{2,1,0,3:T(8,128)} fusion(bf16[1,2,48,4,1024]{4,3,2,1,0:T(4,128)(2,1)S(1)} %copy.305, f32[1,4,256]{2,1,0:T(4,128)S(1)} %get-tuple-element.35, f32[1,4,256]{2,1,0:T(4,128)S(1)} %get-tuple-element.34), kind=kOutput, calls=%fused_computation.122 | convolution fusion | flops 1207963648 | bytes 51126272 | tf_op jit(solution)/shard_map/fcvm,cft->vmt/dot_general | solution.py:27
  401.8 46.6 %fusion.76 = bf16[4,2,48,1024]{3,0,2,1:T(4,128)(2,1)S(1)} fusion(f32[48,1024,256,1]{2,1,0,3:T(8,128)} %fusion.154, s32[48,1024]{1,0:T(8,128)S(1)} %constant_dynamic-slice_fusion.1, f32[1,4,256]{2,1,0:T(4,128)S(1)} %get-tuple-element.35, f32[1,4,256]{2,1,0:T(4,128)S(1)} %get-tuple-element.34), kind=kOutput, calls=%fused_computation.76 | convolution fusion | flops 1233520640 | bytes 51322880 | tf_op jit(solution)/shard_map/vmt,cft->fcvm/dot_general | solution.py:30
  450.0 21.5 %all_to_all.122 = bf16[4,1,2,48,1024]{4,3,2,1,0:T(8,128)(2,1)S(1)} all-to-all(bf16[4,1,2,48,1024]{4,3,2,1,0:T(8,128)(2,1)S(1)} %pad_maximum_fusion.1), channel_id=1, replica_groups=mesh['groups'=2,'freq'=4,'src'=2,'vp'=2] {'freq'}, dimensions={0} | all-to-all | bytes 1572864 | tf_op jit(solution)/shard_map/all_to_all | solution.py:125
  (144 shorter events, 54.1 us)
Async XLA Ops:
  7.2 133.7 %copy-start = (s32[48,4096]{1,0:T(8,128)S(1)}, s32[48,4096]{1,0:T(8,128)}, u32[]{:S(2)}) copy-start(s32[48,4096]{1,0:T(8,128)} %param.11) | copy-start | bytes 2359300
  7.2 50.0 %reduce-scatter.3.cloned.1.call-start = ((), (), s32[]{:S(2)}) async-start(), calls=%async_computation.10 | async-start | bytes 589824 | tf_op jit(solution)/shard_map/reduce_scatter | solution.py:110
  16.3 2.1 copy-start.2
  21.2 2.0 copy-start.4
  23.2 2.1 copy-start.24
  29.2 3.2 copy-start.16
  29.2 3.2 copy-start.17
  29.2 4.8 copy-start.18
  29.2 5.7 %copy-start.19 = (f32[16,48,256]{1,2,0:S(1)}, f32[16,48,256]{1,2,0}, u32[]{:S(2)}) copy-start(f32[16,48,256]{1,2,0} %fusion.161) | copy-start | bytes 2359300
  32.4 5.1 %copy-start.6 = (bf16[1,16,1,32,8,256]{5,4,3,2,1,0:T(8,128)(2,1)}, bf16[1,16,1,32,8,256]{5,4,3,2,1,0:T(8,128)(2,1)S(1)}, u32[]{:S(2)}) copy-start(bf16[1,16,1,32,8,256]{5,4,3,2,1,0:T(8,128)(2,1)S(1)} %get-tuple-element.9) | copy-start | bytes 6291460
  59.9 12.2 %all-to-all-start = ((bf16[4,2,12288]{2,1,0:T(2,128)(2,1)}), bf16[4,2,12288]{2,1,0:T(2,128)(2,1)}, u32[]{:S(2)}, u32[]{:S(2)}) async-start(bf16[4,2,12288]{2,1,0:T(2,128)(2,1)} %reshape.566), calls=%async_computation.1 | async-start | bytes 393216 | tf_op jit(solution)/shard_map/all_to_all | solution.py:113
  93.4 9.7 %all-to-all-start.1 = ((bf16[4,2,48,256]{3,2,1,0:T(8,128)(2,1)}), bf16[4,2,48,256]{3,2,1,0:T(8,128)(2,1)S(1)}, u32[]{:S(2)}, u32[]{:S(2)}) async-start(bf16[4,2,48,256]{3,2,1,0:T(8,128)(2,1)} %copy.260), calls=%async_computation.2 | async-start | bytes 393216 | tf_op jit(solution)/shard_map/all_to_all | solution.py:117
  96.9 3.6 copy-start.20
  103.1 6.6 %copy-start.8 = (bf16[16,32,8,256]{3,1,0,2:T(8,128)(2,1)S(1)}, bf16[16,32,8,256]{3,1,0,2:T(8,128)(2,1)}, u32[]{:S(2)}) copy-start(bf16[16,32,8,256]{3,1,0,2:T(8,128)(2,1)} %copy.265) | copy-start | bytes 6291460
  109.7 1.6 copy-start.10
  113.4 1.6 copy-start.14
  115.8 1.6 copy-start.12
  136.4 21.6 %all-to-all-start.2 = ((bf16[4,2,49152]{2,1,0:T(2,128)(2,1)}), bf16[4,2,49152]{2,1,0:T(2,128)(2,1)}, u32[]{:S(2)}, u32[]{:S(2)}) async-start(bf16[4,2,49152]{2,1,0:T(2,128)(2,1)} %reshape.568), calls=%async_computation.3 | async-start | bytes 1572864 | tf_op jit(solution)/shard_map/all_to_all | solution.py:120
  140.8 144.4 %reduce-scatter.5.cloned.1.call-start = ((), (), s32[]{:S(2)}) async-start(), calls=%async_computation.11 | async-start | bytes 589824 | tf_op jit(solution)/shard_map/reduce_scatter | solution.py:110
  261.1 1.1 copy-start.21
  262.4 1.6 copy-start.3
  264.0 1.6 copy-start.5
  267.7 1.6 copy-start.7
  317.8 16.6 %copy-start.9 = (bf16[16,32,8,256]{3,1,0,2:T(8,128)(2,1)S(1)}, bf16[16,32,8,256]{3,1,0,2:T(8,128)(2,1)}, u32[]{:S(2)}) copy-start(bf16[16,32,8,256]{3,1,0,2:T(8,128)(2,1)} %copy.265) | copy-start | bytes 6291460
  327.9 6.4 %copy-start.23 = (bf16[1,4,2,6,8,256]{5,4,1,3,2,0:T(8,128)(2,1)}, bf16[1,4,2,6,8,256]{5,4,1,3,2,0:T(8,128)(2,1)S(1)}, u32[]{:S(2)}) copy-start(bf16[1,4,2,6,8,256]{5,4,1,3,2,0:T(8,128)(2,1)S(1)} %copy.332) | copy-start | bytes 589828
  334.3 1.6 copy-start.11
  338.0 1.6 copy-start.15
  340.4 1.6 copy-start.13
  471.8 1.1 copy-start.22
  471.8 2.2 copy-start.1
Sparse Core Ops, SparseCore 0:
  41.3 15.7 reduce-scatter.2
  274.0 11.1 reduce-scatter.4
